TPU v7x, 256 devices: a whole 4x4x8 slice. The times are simulated.
256 devices in a mesh: lev: 32 (over y_hi, z, core), pln: 8 (over y_lo, x).
Axes of the slice: x: 4, y: 4 (y_hi: 2, y_lo: 2; y = y_hi * 2 + y_lo), z: 8, core: 2. Of those that a mesh axis runs over, the one named last changes fastest.
Arguments:
- concentration: float32 [128, 1024, 1024], P('lev', 'pln'), may hold values from -2.5 to 2.5
- potential: float32 [1024, 1024], P('pln'), may hold values from -1.5 to 1.5
- lift: float32 [128], replicated, may hold values from 1 to 8
- eigenvalue: float32 [128], replicated, may hold values from 0.05 to 20
- basis: float32 [128, 128], replicated, may hold values from -1 to 2, as said below
- inverse_basis: float32 [128, 128], replicated, may hold values from -1 to 2, as said below
Outputs:
- next_concentration: float32 [128, 1024, 1024], P('lev', 'pln')
Inputs may be any that keep to these rules, and one draw needn't show every extreme that they name: basis times inverse_basis is the identity up to float32 rounding. `inverse_basis`: the matrix inverse of basis, up to float32 rounding.
All inputs are finite; a program needn't handle non-finite values.
Results may differ from a plain program's by a relative error of at most 0.00035.
Values sent between devices are 32-bit elements; how exact they have to be, the bound alone decides.
No kernel may reach another device: no remote copies, remote signals or barrier semaphores. Data moves between devices by JAX's collectives and lax.ppermute only.
A program may use at most 128 MiB of HBM per device.

v0:
```python
import jax
import jax.numpy as jnp
from jax import lax
from jax.sharding import PartitionSpec as P

TIME_STEP = 0.04
GRADIENT_ENERGY = 0.25
EXCHANGE_CURRENT = 0.6


def spread(value, axis, root):
    mine = lax.axis_index(axis) == root
    return lax.psum(jnp.where(mine, value, jnp.zeros_like(value)), axis)


def cas_table(length):
    index = jnp.arange(length, dtype=jnp.int32)
    product = index[:, None] * index[None, :] % length
    angle = product.astype(jnp.float32) * (2.0 * jnp.pi / length)
    return jnp.cos(angle) + jnp.sin(angle)


def wave_squared(index, length):
    folded = jnp.minimum(index, length - index).astype(jnp.float32)
    return (folded * (2.0 * jnp.pi / length)) ** 2


def body(concentration, potential, lift, eigenvalue, basis, inverse_basis):
    highest = lax.Precision.HIGHEST
    lev_count = lax.axis_size("lev")
    pln_count = lax.axis_size("pln")
    lev_index = lax.axis_index("lev")
    pln_index = lax.axis_index("pln")
    own_levels, own_rows, width_y = concentration.shape
    width_x = own_rows * pln_count
    cols_y = width_y // pln_count
    rows_x = width_x // lev_count
    table_x = cas_table(width_x)
    table_y = cas_table(width_y)
    nonlinear = concentration**3 - concentration
    surface = 2.0 * EXCHANGE_CURRENT * jnp.sinh(0.5 * (potential - concentration[0]))
    flux_plane = spread(surface, "lev", 0)
    own_lift = lax.dynamic_slice_in_dim(lift, lev_index * own_levels, own_levels)
    shifted = concentration + TIME_STEP * own_lift[:, None, None] * flux_plane[None]
    stacked = jnp.concatenate([shifted, nonlinear], axis=0)
    along_y = jnp.einsum("lxn,nk->lxk", stacked, table_y, precision=highest)
    spectral = jnp.einsum(
        "kx,lxj->lkj",
        table_x,
        lax.all_to_all(along_y, "pln", split_axis=2, concat_axis=1, tiled=True),
        precision=highest,
    )
    first_modes = spectral[:own_levels]
    second_modes = spectral[own_levels : 2 * own_levels]
    gathered_first, gathered_second = (
        lax.all_to_all(first_modes, "lev", split_axis=1, concat_axis=0, tiled=True),
        lax.all_to_all(second_modes, "lev", split_axis=1, concat_axis=0, tiled=True),
    )
    eigen_first = jnp.einsum("ml,lxy->mxy", inverse_basis, gathered_first, precision=highest)
    eigen_second = jnp.einsum("ml,lxy->mxy", inverse_basis, gathered_second, precision=highest)
    x_index = lev_index * rows_x + jnp.arange(rows_x, dtype=jnp.int32)
    y_index = pln_index * cols_y + jnp.arange(cols_y, dtype=jnp.int32)
    total_wave = wave_squared(x_index, width_x)[:, None] + wave_squared(y_index, width_y)[None, :]
    operator = total_wave[None] + eigenvalue[:, None, None]
    numerator = eigen_first - TIME_STEP * operator * eigen_second
    update = numerator / (1.0 + TIME_STEP * GRADIENT_ENERGY * operator * operator)
    level_values = jnp.einsum("lm,mxy->lxy", basis, update, precision=highest)
    returned = lax.all_to_all(level_values, "lev", split_axis=0, concat_axis=1, tiled=True)
    back_x = jnp.einsum("kx,lxj->lkj", table_x, returned, precision=highest)
    scale_factor = 1.0 / (width_x * width_y)
    return (
        jnp.einsum(
            "lxn,nk->lxk",
            lax.all_to_all(back_x, "pln", split_axis=1, concat_axis=2, tiled=True),
            table_y,
            precision=highest,
        )
        * scale_factor
    )


def solution(mesh):
    in_specs = (P("lev", "pln", None), P("pln", None), P(), P(), P(), P())
    out_specs = P("lev", "pln", None)
    return jax.shard_map(body, mesh=mesh, in_specs=in_specs, out_specs=out_specs, check_vma=False)
```

profile of v0, /device:TPU:32, one launch (start us, length us, event | category | flops | bytes accessed | tf_op | source)
XLA Modules:
  0.0 676.0 jit_solution(15718346257006392588)
XLA Ops:
  9.8 266.7 %all-reduce.2.cloned.1.call-done = f32[128,1024]{1,0:T(8,128)} async-done(((f32[128,1024]{1,0:T(8,128)}), f32[128,1024]{1,0:T(8,128)}) %all-reduce.2.cloned.1.call-update) | async-done | bytes 524304 | tf_op jit(solution)/shard_map/psum | solution.py:13
  279.3 31.3 %fusion.3 = f32[8,128,1024]{2,1,0:T(8,128)} fusion(f32[8,128,1024]{2,1,0:T(8,128)S(1)} %fusion.97), kind=kOutput, calls=%fused_computation.6 | convolution fusion | flops 12900630528 | bytes 8388608 | tf_op jit(solution)/shard_map/lxn,nk->lxk/dot_general | solution.py:46
  310.6 5.4 copy.19
  315.9 4.9 all-to-all-start
  320.9 17.5 %fusion.99 = f32[1024,1024,1]{1,0,2:T(8,128)} fusion(), kind=kLoop, calls=%fused_computation.15.clone.clone.clone.1 | loop fusion | flops 15728640 | bytes 4194304 | tf_op jit(solution)/shard_map/kx,lxj->lkj/dot_general | solution.py:47
  338.4 32.4 %all-to-all-done = f32[8,128,1024]{1,0,2:T(8,128)} async-done(((f32[8,128,1024]{1,0,2:T(8,128)}), f32[8,128,1024]{1,0,2:T(8,128)}, u32[]{:S(2)}, u32[]{:S(2)}) %all-to-all-start) | async-done | bytes 4194336 | tf_op jit(solution)/shard_map/all_to_all | solution.py:50
  370.8 6.6 copy.41
  377.4 4.9 all_to_all.68
  382.3 16.9 %fusion.17 = f32[8,1024,128]{1,2,0:T(8,128)S(1)} fusion(f32[8,1024,128]{1,2,0:T(8,128)} %all_to_all.68, f32[1024,1024,1]{1,0,2:T(8,128)} %fusion.99), kind=kOutput, calls=%fused_computation.26 | convolution fusion | flops 12884901888 | bytes 12582912 | tf_op jit(solution)/shard_map/kx,lxj->lkj/dot_general | solution.py:47
  402.8 9.3 %all-to-all-start.2 = ((f32[4,1024,128]{2,0,1:T(4,128)}), f32[4,1024,128]{2,0,1:T(4,128)S(1)}, u32[]{:S(2)}, u32[]{:S(2)}) async-start(f32[4,1024,128]{2,0,1:T(4,128)} %copy.25), calls=%async_computation.2 | async-start | bytes 4194304 | tf_op jit(solution)/shard_map/all_to_all | solution.py:57
  412.1 2.9 copy.21
  415.0 50.1 %all-to-all-done.2 = f32[4,1024,128]{2,0,1:T(4,128)S(1)} async-done(((f32[4,1024,128]{2,0,1:T(4,128)}), f32[4,1024,128]{2,0,1:T(4,128)S(1)}, u32[]{:S(2)}, u32[]{:S(2)}) %all-to-all-start.2) | async-done | bytes 2097184 | tf_op jit(solution)/shard_map/all_to_all | solution.py:57
  465.1 4.6 all-to-all-start.1
  470.2 51.6 %all-to-all-done.1 = f32[4,1024,128]{2,0,1:T(4,128)} async-done(((f32[4,1024,128]{2,0,1:T(4,128)}), f32[4,1024,128]{2,0,1:T(4,128)}, u32[]{:S(2)}, u32[]{:S(2)}) %all-to-all-start.1) | async-done | bytes 2097184 | tf_op jit(solution)/shard_map/all_to_all | solution.py:56
  523.7 4.3 fusion.24
  528.0 4.3 fusion.26
  536.7 3.8 all-to-all-start.3
  540.5 17.5 %fusion.101 = f32[1024,1024,1]{1,0,2:T(8,128)} fusion(), kind=kLoop, calls=%fused_computation.13.clone.clone.clone.1 | loop fusion | flops 15728640 | bytes 4194304 | tf_op jit(solution)/shard_map/kx,lxj->lkj/dot_general | solution.py:69
  558.0 35.1 %all-to-all-done.3 = f32[128,32,128]{2,1,0:T(8,128)S(1)} async-done(((f32[128,32,128]{2,1,0:T(8,128)}), f32[128,32,128]{2,1,0:T(8,128)S(1)}, u32[]{:S(2)}, u32[]{:S(2)}) %all-to-all-start.3) | async-done | bytes 2097184 | tf_op jit(solution)/shard_map/all_to_all | solution.py:68
  595.3 13.7 %fusion.33 = f32[4,1024,128]{1,2,0:T(8,128)S(1)} fusion(f32[4,1024,128]{2,1,0:T(8,128)S(1)} %bitcast.103, f32[1024,1024,1]{1,0,2:T(8,128)S(1)} %copy-done.1), kind=kOutput, calls=%fused_computation.39 | convolution fusion | flops 6442450944 | bytes 8388608 | tf_op jit(solution)/shard_map/kx,lxj->lkj/dot_general | solution.py:69
  610.8 17.6 %all-to-all-start.4 = ((f32[4,1024,128]{2,0,1:T(4,128)}), f32[4,1024,128]{2,0,1:T(4,128)S(1)}, u32[]{:S(2)}, u32[]{:S(2)}) async-start(f32[4,1024,128]{2,0,1:T(4,128)} %copy.32), calls=%async_computation.4 | async-start | bytes 4194304 | tf_op jit(solution)/shard_map/all_to_all | solution.py:74
  628.4 17.5 %fusion.103 = f32[1024,1024,1]{1,0,2:T(8,128)} fusion(), kind=kLoop, calls=%fused_computation.11.clone.clone.clone.1 | loop fusion | flops 15728640 | bytes 4194304 | tf_op jit(solution)/shard_map/lxn,nk->lxk/dot_general | solution.py:72
  645.9 9.1 %all-to-all-done.4 = f32[4,1024,128]{2,0,1:T(4,128)S(1)} async-done(((f32[4,1024,128]{2,0,1:T(4,128)}), f32[4,1024,128]{2,0,1:T(4,128)S(1)}, u32[]{:S(2)}, u32[]{:S(2)}) %all-to-all-start.4) | async-done | bytes 2097184 | tf_op jit(solution)/shard_map/all_to_all | solution.py:74
  659.3 9.6 %fusion.36 = f32[4,128,1024]{2,1,0:T(8,128)} fusion(f32[4,128,1024]{2,1,0:T(8,128)S(1)} %all_to_all.84, f32[1024,1024,1]{1,0,2:T(8,128)} %fusion.103), kind=kOutput, calls=%fused_computation.40 | convolution fusion | flops 6442975232 | bytes 8388608 | tf_op jit(solution)/shard_map/lxn,nk->lxk/dot_general | solution.py:72
  (29 shorter events, 24.7 us)
Async XLA Ops:
  6.5 517.2 %copy-start = (f32[128,128]{1,0:T(8,128)S(1)}, f32[128,128]{1,0:T(8,128)}, u32[]{:S(2)}) copy-start(f32[128,128]{1,0:T(8,128)} %param.11) | copy-start | bytes 196612
  6.5 269.9 %all-reduce.2.cloned.1.call-start = ((), (), s32[]{:S(2)}) async-start(), calls=%async_computation.5 | async-start | bytes 1048576 | tf_op jit(solution)/shard_map/psum | solution.py:13
  315.9 54.8 %all-to-all-start = ((f32[8,128,1024]{1,0,2:T(8,128)}), f32[8,128,1024]{1,0,2:T(8,128)}, u32[]{:S(2)}, u32[]{:S(2)}) async-start(f32[8,128,1024]{1,0,2:T(8,128)} %copy.19), calls=%async_computation | async-start | bytes 8388608 | tf_op jit(solution)/shard_map/all_to_all | solution.py:50
  402.8 62.3 %all-to-all-start.2 = ((f32[4,1024,128]{2,0,1:T(4,128)}), f32[4,1024,128]{2,0,1:T(4,128)S(1)}, u32[]{:S(2)}, u32[]{:S(2)}) async-start(f32[4,1024,128]{2,0,1:T(4,128)} %copy.25), calls=%async_computation.2 | async-start | bytes 4194304 | tf_op jit(solution)/shard_map/all_to_all | solution.py:57
  465.1 56.6 %all-to-all-start.1 = ((f32[4,1024,128]{2,0,1:T(4,128)}), f32[4,1024,128]{2,0,1:T(4,128)}, u32[]{:S(2)}, u32[]{:S(2)}) async-start(f32[4,1024,128]{2,0,1:T(4,128)} %copy.21), calls=%async_computation.1 | async-start | bytes 4194304 | tf_op jit(solution)/shard_map/all_to_all | solution.py:56
  523.7 8.6 %copy-start.2 = (f32[128,128]{1,0:T(8,128)S(1)}, f32[128,128]{1,0:T(8,128)}, u32[]{:S(2)}) copy-start(f32[128,128]{1,0:T(8,128)} %param.10) | copy-start | bytes 196612
  523.7 8.6 %copy-start.3 = (f32[128]{0:T(128)S(1)}, f32[128]{0:T(128)}, u32[]{:S(2)}) copy-start(f32[128]{0:T(128)} %param.9) | copy-start | bytes 1540
  536.7 56.4 %all-to-all-start.3 = ((f32[128,32,128]{2,1,0:T(8,128)}), f32[128,32,128]{2,1,0:T(8,128)S(1)}, u32[]{:S(2)}, u32[]{:S(2)}) async-start(f32[128,32,128]{2,1,0:T(8,128)} %copy.29), calls=%async_computation.3 | async-start | bytes 4194304 | tf_op jit(solution)/shard_map/all_to_all | solution.py:68
  593.1 2.2 copy-start.1
  610.8 44.2 %all-to-all-start.4 = ((f32[4,1024,128]{2,0,1:T(4,128)}), f32[4,1024,128]{2,0,1:T(4,128)S(1)}, u32[]{:S(2)}, u32[]{:S(2)}) async-start(f32[4,1024,128]{2,0,1:T(4,128)} %copy.32), calls=%async_computation.4 | async-start | bytes 4194304 | tf_op jit(solution)/shard_map/all_to_all | solution.py:74
Sparse Core Ops, SparseCore 0:
  9.9 266.4 all-reduce.1
where the time goes:
time: 684 us; the launch traced here: 676 us
  waiting for transfers between devices  445 us (65%)
  matrix products  82.2 us (12%)
  other arithmetic  58.7 us (9%)
  starting transfers between devices  40.1 us (6%)
  local copies, waits for them, and re-layouts  36.1 us (5%)
  between operations  13.8 us (2%)
    psum x1, waiting for transfers between devices, spread(): return lax.psum(jnp.where(mine, value, jnp.zeros_like(value)), axis)  267 us
    all_to_all x1, waiting for transfers between devices, body(): lax.all_to_all(first_modes, 'lev', split_axis=1, concat_axis=0, tiled=True)  51.6 us
    all_to_all x1, waiting for transfers between devices, body(): lax.all_to_all(second_modes, 'lev', split_axis=1, concat_axis=0, tiled=True)  50.1 us
    all_to_all x1, waiting for transfers between devices, body(): lax.all_to_all(level_values, 'lev', split_axis=0, concat_axis=1, tiled=True)  35.1 us
    all_to_all x1, waiting for transfers between devices, body(): lax.all_to_all(along_y, 'pln', split_axis=2, concat_axis=1, tiled=True)  32.4 us
    dot_general x1, matrix products, body(): along_y = jnp.einsum('lxn,nk->lxk', stacked, table_y, precision=highest)  31.3 us
    all_to_all x1, starting transfers between devices, body(): lax.all_to_all(back_x, 'pln', split_axis=1, concat_axis=2, tiled=True)  17.6 us
    dot_general x1, other arithmetic, body(): back_x = jnp.einsum('kx,lxj->lkj', table_x, returned, precision=highest)  17.5 us
  transfers between devices with their start and end apart: 6, of which 6 were waited for; matrix products, arithmetic and copies ran while one was open for 8% of the time, Pallas kernels for 0%

commit v1 on v0

--- a/solution.py
+++ b/solution.py
@@ -10,7 +10,7 @@
 
 def spread(value, axis, root):
     mine = lax.axis_index(axis) == root
-    return lax.psum(jnp.where(mine, value, jnp.zeros_like(value)), axis)
+    return jnp.sum(lax.all_gather(jnp.where(mine, value, jnp.zeros_like(value)), axis), axis=0)
 
 
 def cas_table(length):

time: 684 us -> 569 us (0.83)
  waiting for transfers between devices: 445 us -> 317 us
    psum x1 -> x0, waiting for transfers between devices: 267 us -> none  [spread(): return lax.psum(jnp.where(mine, value, jnp.zeros_like(value)), axis)]
    all_gather x0 -> x1, waiting for transfers between devices: none -> 138 us  [spread(): lax.all_gather(jnp.where(mine, value, jnp.zeros_like(value)), axis)]
    reduce_sum x0 -> x1, other arithmetic: none -> 7.6 us  [spread(): jnp.sum(lax.all_gather(jnp.where(mine, value, jnp.zeros_like(value)), axi...]
  transfers between devices with their start and end apart: 6 -> 6, of which waited for: 6 -> 6; matrix products, arithmetic and copies ran while one was open for 8% -> 10% of each run, Pallas kernels for 0% -> 0%
where the time goes in v1:
time: 569 us; the launch traced here: 560 us
  waiting for transfers between devices  317 us (56%)
  matrix products  82.3 us (14%)
  other arithmetic  64.6 us (11%)
  starting transfers between devices  46.1 us (8%)
  local copies, waits for them, and re-layouts  36.2 us (6%)
  between operations  14 us (2%)
    all_gather x1, waiting for transfers between devices, spread(): lax.all_gather(jnp.where(mine, value, jnp.zeros_like(value)), axis)  138 us
    all_to_all x1, waiting for transfers between devices, body(): lax.all_to_all(first_modes, 'lev', split_axis=1, concat_axis=0, tiled=True)  51.6 us
    all_to_all x1, waiting for transfers between devices, body(): lax.all_to_all(second_modes, 'lev', split_axis=1, concat_axis=0, tiled=True)  50.1 us
    all_to_all x1, waiting for transfers between devices, body(): lax.all_to_all(level_values, 'lev', split_axis=0, concat_axis=1, tiled=True)  35.1 us
    all_to_all x1, waiting for transfers between devices, body(): lax.all_to_all(along_y, 'pln', split_axis=2, concat_axis=1, tiled=True)  32.6 us
    dot_general x1, matrix products, body(): along_y = jnp.einsum('lxn,nk->lxk', stacked, table_y, precision=highest)  31.2 us
    all_to_all x1, starting transfers between devices, body(): lax.all_to_all(back_x, 'pln', split_axis=1, concat_axis=2, tiled=True)  17.8 us
    dot_general x1, other arithmetic, body(): jnp.einsum('kx,lxj->lkj', table_x, lax.all_to_all(along_y, 'pln', split_a...  17.5 us
  transfers between devices with their start and end apart: 6, of which 6 were waited for; matrix products, arithmetic and copies ran while one was open for 10% of the time, Pallas kernels for 0%

profile of v1, /device:TPU:32, one launch (start us, length us, event | category | flops | bytes accessed | tf_op | source)
XLA Modules:
  0.0 560.1 jit_solution(1449192944733971212)
XLA Ops:
  9.8 138.3 %all-gather.3.cloned.1.call-done = f32[4096,1024]{1,0:T(8,128)} async-done(((f32[128,1024]{1,0:T(8,128)}), f32[4096,1024]{1,0:T(8,128)}) %all-gather.3.cloned.1.call-update) | async-done | bytes 16777232 | tf_op jit(solution)/shard_map/all_gather | solution.py:13
  148.1 7.6 %reduce_sum.9 = f32[128,1024]{1,0:T(8,128)S(1)} reduce(f32[32,128,1024]{2,1,0:T(8,128)} %bitcast.96, f32[]{:T(128)} %constant.15.clone.1), dimensions={0}, to_apply=%region_0.1 | reduce | flops 4063232 | bytes 17301508 | tf_op jit(solution)/shard_map/reduce_sum | solution.py:13
  156.9 31.2 %fusion.3 = f32[8,128,1024]{2,1,0:T(8,128)} fusion(f32[8,128,1024]{2,1,0:T(8,128)S(1)} %fusion.97), kind=kOutput, calls=%fused_computation.6 | convolution fusion | flops 12900630528 | bytes 8388608 | tf_op jit(solution)/shard_map/lxn,nk->lxk/dot_general | solution.py:46
  188.1 5.4 copy.19
  193.5 4.8 all-to-all-start
  198.3 17.5 %fusion.99 = f32[1024,1024,1]{1,0,2:T(8,128)} fusion(), kind=kLoop, calls=%fused_computation.15.clone.clone.clone.1 | loop fusion | flops 15728640 | bytes 4194304 | tf_op jit(solution)/shard_map/kx,lxj->lkj/dot_general | solution.py:47
  215.8 32.6 %all-to-all-done = f32[8,128,1024]{1,0,2:T(8,128)} async-done(((f32[8,128,1024]{1,0,2:T(8,128)}), f32[8,128,1024]{1,0,2:T(8,128)}, u32[]{:S(2)}, u32[]{:S(2)}) %all-to-all-start) | async-done | bytes 4194336 | tf_op jit(solution)/shard_map/all_to_all | solution.py:50
  248.5 6.6 %copy.41 = f32[8,128,8,128]{1,2,3,0:T(8,128)} copy(f32[8,128,8,128]{1,0,3,2:T(8,128)} %bitcast.3) | data formatting | bytes 8388608 | tf_op jit(solution)/shard_map/all_to_all | solution.py:50
  255.1 4.9 all_to_all.68
  260.0 16.9 %fusion.17 = f32[8,1024,128]{1,2,0:T(8,128)S(1)} fusion(f32[8,1024,128]{1,2,0:T(8,128)} %all_to_all.68, f32[1024,1024,1]{1,0,2:T(8,128)} %fusion.99), kind=kOutput, calls=%fused_computation.26 | convolution fusion | flops 12884901888 | bytes 12582912 | tf_op jit(solution)/shard_map/kx,lxj->lkj/dot_general | solution.py:47
  280.5 15.1 %all-to-all-start.2 = ((f32[4,1024,128]{2,0,1:T(4,128)}), f32[4,1024,128]{2,0,1:T(4,128)S(1)}, u32[]{:S(2)}, u32[]{:S(2)}) async-start(f32[4,1024,128]{2,0,1:T(4,128)} %copy.25), calls=%async_computation.2 | async-start | bytes 4194304 | tf_op jit(solution)/shard_map/all_to_all | solution.py:57
  298.6 50.1 %all-to-all-done.2 = f32[4,1024,128]{2,0,1:T(4,128)S(1)} async-done(((f32[4,1024,128]{2,0,1:T(4,128)}), f32[4,1024,128]{2,0,1:T(4,128)S(1)}, u32[]{:S(2)}, u32[]{:S(2)}) %all-to-all-start.2) | async-done | bytes 2097184 | tf_op jit(solution)/shard_map/all_to_all | solution.py:57
  348.7 4.6 all-to-all-start.1
  353.7 51.6 %all-to-all-done.1 = f32[4,1024,128]{2,0,1:T(4,128)} async-done(((f32[4,1024,128]{2,0,1:T(4,128)}), f32[4,1024,128]{2,0,1:T(4,128)}, u32[]{:S(2)}, u32[]{:S(2)}) %all-to-all-start.1) | async-done | bytes 2097184 | tf_op jit(solution)/shard_map/all_to_all | solution.py:56
  407.3 4.3 fusion.24
  411.6 4.3 fusion.26
  420.3 3.8 all-to-all-start.3
  424.1 17.5 %fusion.101 = f32[1024,1024,1]{1,0,2:T(8,128)} fusion(), kind=kLoop, calls=%fused_computation.13.clone.clone.clone.1 | loop fusion | flops 15728640 | bytes 4194304 | tf_op jit(solution)/shard_map/kx,lxj->lkj/dot_general | solution.py:69
  441.7 35.1 %all-to-all-done.3 = f32[128,32,128]{2,1,0:T(8,128)S(1)} async-done(((f32[128,32,128]{2,1,0:T(8,128)}), f32[128,32,128]{2,1,0:T(8,128)S(1)}, u32[]{:S(2)}, u32[]{:S(2)}) %all-to-all-start.3) | async-done | bytes 2097184 | tf_op jit(solution)/shard_map/all_to_all | solution.py:68
  478.9 13.7 %fusion.33 = f32[4,1024,128]{1,2,0:T(8,128)S(1)} fusion(f32[4,1024,128]{2,1,0:T(8,128)S(1)} %bitcast.105, f32[1024,1024,1]{1,0,2:T(8,128)S(1)} %copy-done.1), kind=kOutput, calls=%fused_computation.39 | convolution fusion | flops 6442450944 | bytes 8388608 | tf_op jit(solution)/shard_map/kx,lxj->lkj/dot_general | solution.py:69
  494.5 17.8 %all-to-all-start.4 = ((f32[4,1024,128]{2,0,1:T(4,128)}), f32[4,1024,128]{2,0,1:T(4,128)S(1)}, u32[]{:S(2)}, u32[]{:S(2)}) async-start(f32[4,1024,128]{2,0,1:T(4,128)} %copy.32), calls=%async_computation.4 | async-start | bytes 4194304 | tf_op jit(solution)/shard_map/all_to_all | solution.py:74
  512.3 17.5 %fusion.103 = f32[1024,1024,1]{1,0,2:T(8,128)} fusion(), kind=kLoop, calls=%fused_computation.11.clone.clone.clone.1 | loop fusion | flops 15728640 | bytes 4194304 | tf_op jit(solution)/shard_map/lxn,nk->lxk/dot_general | solution.py:72
  529.8 9.1 %all-to-all-done.4 = f32[4,1024,128]{2,0,1:T(4,128)S(1)} async-done(((f32[4,1024,128]{2,0,1:T(4,128)}), f32[4,1024,128]{2,0,1:T(4,128)S(1)}, u32[]{:S(2)}, u32[]{:S(2)}) %all-to-all-start.4) | async-done | bytes 2097184 | tf_op jit(solution)/shard_map/all_to_all | solution.py:74
  543.2 9.6 %fusion.36 = f32[4,128,1024]{2,1,0:T(8,128)} fusion(f32[4,128,1024]{2,1,0:T(8,128)S(1)} %all_to_all.84, f32[1024,1024,1]{1,0,2:T(8,128)} %fusion.103), kind=kOutput, calls=%fused_computation.40 | convolution fusion | flops 6442975232 | bytes 8388608 | tf_op jit(solution)/shard_map/lxn,nk->lxk/dot_general | solution.py:72
  (32 shorter events, 26.0 us)
Async XLA Ops:
  6.5 400.8 %copy-start = (f32[128,128]{1,0:T(8,128)S(1)}, f32[128,128]{1,0:T(8,128)}, u32[]{:S(2)}) copy-start(f32[128,128]{1,0:T(8,128)} %param.11) | copy-start | bytes 196612
  6.5 141.6 %all-gather.3.cloned.1.call-start = ((), (), s32[]{:S(2)}) async-start(), calls=%async_computation.5 | async-start | bytes 17301504 | tf_op jit(solution)/shard_map/all_gather | solution.py:13
  148.1 7.6 %copy-start.2 = (f32[4,128,1024]{2,1,0:T(8,128)S(1)}, f32[4,128,1024]{2,1,0:T(8,128)}, u32[]{:S(2)}) copy-start(f32[4,128,1024]{2,1,0:T(8,128)} %param.6) | copy-start | bytes 6291460
  193.5 55.0 %all-to-all-start = ((f32[8,128,1024]{1,0,2:T(8,128)}), f32[8,128,1024]{1,0,2:T(8,128)}, u32[]{:S(2)}, u32[]{:S(2)}) async-start(f32[8,128,1024]{1,0,2:T(8,128)} %copy.19), calls=%async_computation | async-start | bytes 8388608 | tf_op jit(solution)/shard_map/all_to_all | solution.py:50
  280.5 68.2 %all-to-all-start.2 = ((f32[4,1024,128]{2,0,1:T(4,128)}), f32[4,1024,128]{2,0,1:T(4,128)S(1)}, u32[]{:S(2)}, u32[]{:S(2)}) async-start(f32[4,1024,128]{2,0,1:T(4,128)} %copy.25), calls=%async_computation.2 | async-start | bytes 4194304 | tf_op jit(solution)/shard_map/all_to_all | solution.py:57
  348.7 56.6 %all-to-all-start.1 = ((f32[4,1024,128]{2,0,1:T(4,128)}), f32[4,1024,128]{2,0,1:T(4,128)}, u32[]{:S(2)}, u32[]{:S(2)}) async-start(f32[4,1024,128]{2,0,1:T(4,128)} %copy.21), calls=%async_computation.1 | async-start | bytes 4194304 | tf_op jit(solution)/shard_map/all_to_all | solution.py:56
  407.3 8.6 %copy-start.3 = (f32[128,128]{1,0:T(8,128)S(1)}, f32[128,128]{1,0:T(8,128)}, u32[]{:S(2)}) copy-start(f32[128,128]{1,0:T(8,128)} %param.10) | copy-start | bytes 196612
  407.3 8.6 %copy-start.4 = (f32[128]{0:T(128)S(1)}, f32[128]{0:T(128)}, u32[]{:S(2)}) copy-start(f32[128]{0:T(128)} %param.9) | copy-start | bytes 1540
  420.3 56.4 %all-to-all-start.3 = ((f32[128,32,128]{2,1,0:T(8,128)}), f32[128,32,128]{2,1,0:T(8,128)S(1)}, u32[]{:S(2)}, u32[]{:S(2)}) async-start(f32[128,32,128]{2,1,0:T(8,128)} %copy.29), calls=%async_computation.3 | async-start | bytes 4194304 | tf_op jit(solution)/shard_map/all_to_all | solution.py:68
  476.7 2.2 copy-start.1
  494.5 44.5 %all-to-all-start.4 = ((f32[4,1024,128]{2,0,1:T(4,128)}), f32[4,1024,128]{2,0,1:T(4,128)S(1)}, u32[]{:S(2)}, u32[]{:S(2)}) async-start(f32[4,1024,128]{2,0,1:T(4,128)} %copy.32), calls=%async_computation.4 | async-start | bytes 4194304 | tf_op jit(solution)/shard_map/all_to_all | solution.py:74
Sparse Core Ops, SparseCore 0:
  10.1 137.9 all-gather.2
